TPU v7x, 32 devices: a whole 2x2x4 slice. The times are simulated.
32 devices in a mesh: ep: 8 (over z, x), tp: 4 (over y, core).
Axes of the slice: x: 2, y: 2, z: 4, core: 2. Of those that a mesh axis runs over, the one named last changes fastest.
Arguments:
- features: bfloat16 [2048, 1024], P('ep'), may hold values from -6 to 6
- cotangent: bfloat16 [2048, 2048], P('ep'), may hold values from -6 to 6
- expert_ids: int32 [2048, 2], P('ep'), may hold values from 0 to 7, all different within a row; in each aligned block of 256 rows (0 to 255, 256 to 511, ...) at most 96 rows name the same one
- gate_levels: int32 [2048, 2], P('ep'), may hold values from 1 to 15
- w_in: bfloat16 [8, 1024, 4096], P('ep', None, 'tp'), may hold values from -0.1875 to 0.1875
- w_out: bfloat16 [8, 4096, 2048], P('ep', 'tp'), may hold values from -0.09375 to 0.09375
Outputs:
- grad_in: bfloat16 [2048, 1024], P('ep', 'tp')
- grad_w_in: bfloat16 [8, 1024, 4096], P('ep', None, 'tp')
- grad_w_out: bfloat16 [8, 4096, 2048], P('ep', 'tp')
Inputs may be any that keep to these rules, and one draw needn't show every extreme that they name: `expert_ids`: each row names two different experts. In each aligned block of 256 rows no expert is named by more than 96 rows, and some expert reaches 96 rows in some block.
All inputs are finite; a program needn't handle non-finite values.
Results may differ from a plain program's by a relative error of at most 0.0065.
Values may be sent and summed in bfloat16 or wider, within the bound.
No kernel may reach another device: no remote copies, remote signals or barrier semaphores. Data moves between devices by JAX's collectives and lax.ppermute only.
A program may use at most 128 MiB of HBM per device.

v0:
```python
import math
import jax
import jax.numpy as jnp
from jax import lax
from jax.sharding import PartitionSpec as P

E = 8


def shifted(value, axis, by):
    peers = lax.axis_size(axis)
    return lax.ppermute(value, axis, [(i, (i + by) % peers) for i in range(peers)])


def slot_positions(expert_ids, blocks, experts, capacity):
    flattened = expert_ids.reshape(blocks, -1)
    one_hot = (flattened[:, :, None] == jnp.arange(experts, dtype=jnp.int32)[None, None, :]).astype(
        jnp.int32
    )
    earlier = jnp.cumsum(one_hot, axis=1) - one_hot
    within = jnp.sum(one_hot * earlier, axis=2)
    block_ids = jnp.arange(blocks, dtype=jnp.int32)[:, None]
    return ((block_ids * experts + flattened) * capacity + within).reshape(-1)


def shards(features, cotangent, expert_ids, gate_levels, w_in, w_out):
    device_count = lax.axis_size("ep")
    replicas = device_count // E
    replica = lax.axis_index("ep") // E
    tokens_here = expert_ids.shape[0]
    sub_rows = tokens_here // replicas
    capacity = 3 * sub_rows // 8
    slot_count = device_count * capacity
    pair_count = 2 * tokens_here
    positions = slot_positions(expert_ids, replicas, E, capacity)
    owner = (
        jnp.full((slot_count,), pair_count, jnp.int32)
        .at[positions]
        .set(jnp.arange(pair_count, dtype=jnp.int32))
    )
    filled = owner < pair_count
    pair_ids = jnp.minimum(owner, pair_count - 1)
    token_ids = pair_ids // 2
    gate_values = gate_levels.reshape(-1).astype(jnp.float32) / 16.0
    slot_gates = jnp.where(filled, gate_values[pair_ids], 0.0)
    slot_mask = filled.astype(jnp.bfloat16)[:, None]
    packed_x = features[token_ids] * slot_mask
    packed_dy = (cotangent[token_ids].astype(jnp.float32) * slot_gates[:, None]).astype(
        jnp.bfloat16
    )
    rows_x, rows_dy = (
        lax.all_to_all(packed_x, "ep", split_axis=0, concat_axis=0, tiled=True),
        lax.all_to_all(packed_dy, "ep", split_axis=0, concat_axis=0, tiled=True),
    )
    piece_in = w_in[0]
    piece_out = w_out[0]
    span = piece_in.shape[1]
    weight_in = jnp.zeros((piece_in.shape[0], span * replicas), jnp.bfloat16)
    weight_out = jnp.zeros((span * replicas, piece_out.shape[1]), jnp.bfloat16)
    weight_in = lax.dynamic_update_slice_in_dim(weight_in, piece_in, replica * span, 1)
    weight_out = lax.dynamic_update_slice_in_dim(weight_out, piece_out, replica * span, 0)
    moving = (piece_in, piece_out)
    for turn_index in range(1, replicas):
        moving = shifted((moving[0], moving[1]), "ep", E)
        anchor = (replica - turn_index) % replicas
        weight_in = lax.dynamic_update_slice_in_dim(weight_in, moving[0], anchor * span, 1)
        weight_out = lax.dynamic_update_slice_in_dim(weight_out, moving[1], anchor * span, 0)
    pre = jnp.dot(rows_x, weight_in, preferred_element_type=jnp.float32)
    activated, gelu_back = jax.vjp(jax.nn.gelu, pre)
    act_rows = activated.astype(jnp.bfloat16)
    back_act = lax.dot_general(
        rows_dy, weight_out, (((1,), (1,)), ((), ())), preferred_element_type=jnp.float32
    )
    back_pre = gelu_back(back_act)[0].astype(jnp.bfloat16)
    summed = lax.psum_scatter(
        lax.dot_general(
            weight_in, back_pre, (((1,), (1,)), ((), ())), preferred_element_type=jnp.float32
        ),
        "tp",
        scatter_dimension=0,
        tiled=True,
    )
    returned = lax.all_to_all(
        summed.astype(jnp.bfloat16), "ep", split_axis=1, concat_axis=1, tiled=True
    )
    picked = returned[:, positions].astype(jnp.float32)
    grad_in = jnp.sum(picked.reshape(picked.shape[0], tokens_here, 2), axis=2).T.astype(
        jnp.bfloat16
    )

    def span_grads(first_span, span_total):
        width = span_total * span
        act_cols = lax.dynamic_slice_in_dim(act_rows, first_span * span, width, 1)
        pre_cols = lax.dynamic_slice_in_dim(back_pre, first_span * span, width, 1)
        grad_first = lax.dot_general(
            pre_cols, rows_x, (((0,), (0,)), ((), ())), preferred_element_type=jnp.float32
        )
        grad_second = lax.dot_general(
            act_cols, rows_dy, (((0,), (0,)), ((), ())), preferred_element_type=jnp.float32
        )
        return (grad_first, grad_second)

    summed_grads = span_grads((replica - 1) % replicas, 1)
    for turn_index in range(1, replicas):
        summed_grads = shifted((summed_grads[0], summed_grads[1]), "ep", E)
        own_grads = span_grads((replica - turn_index - 1) % replicas, 1)
        summed_grads = (summed_grads[0] + own_grads[0], summed_grads[1] + own_grads[1])
    grad_scale = 1.0 / math.sqrt(2.0 * tokens_here * device_count / E)
    grad_w_in = (summed_grads[0] * grad_scale).T.astype(jnp.bfloat16)[None]
    grad_w_out = (summed_grads[1] * grad_scale).astype(jnp.bfloat16)[None]
    return (grad_in, grad_w_in, grad_w_out)


def solution(mesh):
    return jax.shard_map(
        shards,
        mesh=mesh,
        in_specs=(
            P("ep", None),
            P("ep", None),
            P("ep", None),
            P("ep", None),
            P("ep", None, "tp"),
            P("ep", "tp", None),
        ),
        out_specs=(P("ep", "tp"), P("ep", None, "tp"), P("ep", "tp", None)),
        check_vma=False,
    )
```

profile of v0, /device:TPU:0, one launch (start us, length us, event | category | flops | bytes accessed | tf_op | source)
XLA Modules:
  0.0 224.9 jit_solution(1685540654432374637)
XLA Ops:
  7.2 1.0 copy.10
  8.2 0.7 broadcast_multiply_fusion.1
  8.9 0.1 eq.29
  9.0 1.1 reduce-window.6
  10.2 0.2 slice_reduce_fusion
  10.5 0.1 copy.9
  10.6 0.1 mul.109
  10.8 2.4 %scatter_custom_fusion = s32[768]{0:T(1024)S(1)} fusion(s32[512]{0:T(512)S(1)} %bitcast.57, s32[512]{0:T(512)S(1)} %iota.15, s32[]{:T(128)} %constant.26.clone.1), kind=kCustom, calls=%fused_computation.57 | custom fusion | bytes 3076 | tf_op jit(solution)/shard_map/scatter | solution.py:39
  13.3 0.7 convert_multiply_fusion.1
  14.1 0.1 div.25
  14.3 5.0 %gather_fusion.1 = f32[768]{0:T(1024)S(1)} fusion(f32[512]{0:T(512)S(1)} %div.25, s32[1024]{0:T(1024)S(1)} %get-tuple-element.7), kind=kCustom, calls=%fused_computation.1 | custom fusion | bytes 9216 | tf_op jit(solution)/shard_map/gather | solution.py:45
  19.4 3.5 %gather_fusion.2 = bf16[768,1024]{1,0:T(8,128)(2,1)} fusion(bf16[256,1024]{1,0:T(8,128)(2,1)S(1)} %copy-done.2, s32[1024]{0:T(1024)S(1)} %get-tuple-element.8), kind=kCustom, calls=%fused_computation.2 | custom fusion | bytes 3148800 | tf_op jit(solution)/shard_map/gather | solution.py:47
  23.0 2.8 %broadcast_multiply_fusion = bf16[8,96,1024]{2,1,0:T(8,128)(2,1)} fusion(bf16[8,96,1024]{2,1,0:T(8,128)(2,1)} %bitcast.54, bf16[8,96]{1,0:T(8,128)(2,1)S(1)} %reshape.196), kind=kLoop, calls=%fused_computation.32 | loop fusion | flops 786432 | bytes 3147264 | tf_op jit(solution)/shard_map/mul | solution.py:47
  25.8 7.3 %all-to-all-start.1 = ((bf16[8,96,1024]{2,1,0:T(8,128)(2,1)}), bf16[8,96,1024]{2,1,0:T(8,128)(2,1)}, u32[]{:S(2)}, u32[]{:S(2)}) async-start(bf16[8,96,1024]{2,1,0:T(8,128)(2,1)} %broadcast_multiply_fusion), calls=%async_computation.1 | async-start | bytes 3145728 | tf_op jit(solution)/shard_map/all_to_all | solution.py:52
  33.1 4.2 %gather_fusion = bf16[768,2048]{1,0:T(8,128)(2,1)} fusion(bf16[256,2048]{1,0:T(8,128)(2,1)S(1)} %copy-done.1, s32[1024]{0:T(1024)S(1)} %get-tuple-element.8), kind=kCustom, calls=%fused_computation | custom fusion | bytes 6294528 | tf_op jit(solution)/shard_map/gather | solution.py:48
  37.4 4.1 %fusion = bf16[8,96,2048]{2,1,0:T(8,128)(2,1)} fusion(bf16[8,96,2048]{2,1,0:T(8,128)(2,1)} %bitcast.53, f32[8,96]{1,0:T(8,128)S(1)} %mul.111), kind=kLoop, calls=%fused_computation.7 | loop fusion | flops 4718592 | bytes 6294528 | tf_op jit(solution)/shard_map/convert_element_type | solution.py:48
  41.5 28.7 %all-to-all-done.1 = bf16[8,96,1024]{2,1,0:T(8,128)(2,1)} async-done(((bf16[8,96,1024]{2,1,0:T(8,128)(2,1)}), bf16[8,96,1024]{2,1,0:T(8,128)(2,1)}, u32[]{:S(2)}, u32[]{:S(2)}) %all-to-all-start.1) | async-done | bytes 1572896 | tf_op jit(solution)/shard_map/all_to_all | solution.py:52
  70.2 4.4 %all-to-all-start = ((bf16[8,96,2048]{2,1,0:T(8,128)(2,1)}), bf16[8,96,2048]{2,1,0:T(8,128)(2,1)}, u32[]{:S(2)}, u32[]{:S(2)}) async-start(bf16[8,96,2048]{2,1,0:T(8,128)(2,1)} %fusion), calls=%async_computation | async-start | bytes 6291456 | tf_op jit(solution)/shard_map/all_to_all | solution.py:53
  74.6 0.2 reduce-scatter.2.cloned.1.call-start
  74.9 4.9 %fusion.15 = f32[768,1024]{1,0:T(8,128)} fusion(bf16[768,1024]{1,0:T(8,128)(2,1)} %bitcast.12, bf16[1,1024,1024]{2,1,0:T(8,128)(2,1)S(1)} %copy-done), kind=kOutput, calls=%fused_computation.24 | convolution fusion | flops 1610612736 | bytes 6815744 | tf_op jit(solution)/shard_map/dot_general | solution.py:68
  79.8 65.1 %all-to-all-done = bf16[8,96,2048]{2,1,0:T(8,128)(2,1)} async-done(((bf16[8,96,2048]{2,1,0:T(8,128)(2,1)}), bf16[8,96,2048]{2,1,0:T(8,128)(2,1)}, u32[]{:S(2)}, u32[]{:S(2)}) %all-to-all-start) | async-done | bytes 3145760 | tf_op jit(solution)/shard_map/all_to_all | solution.py:53
  144.8 9.1 %fusion.10 = bf16[768,1024]{1,0:T(8,128)(2,1)S(1)} fusion(f32[768,1024]{1,0:T(8,128)} %fusion.15, bf16[768,2048]{1,0:T(8,128)(2,1)} %bitcast.9, bf16[1,1024,2048]{2,1,0:T(8,128)(2,1)} %param.11), kind=kOutput, calls=%fused_computation.20 | convolution fusion | flops 3236954112 | bytes 12058624 | tf_op jit(solution)/shard_map/dot_general | solution.py:71
  153.9 1.2 copy-done.3
  155.2 3.5 %fusion.17 = f32[1024,768]{0,1:T(8,128)} fusion(bf16[768,1024]{1,0:T(8,128)(2,1)S(1)} %fusion.10, bf16[1,1024,1024]{2,1,0:T(8,128)(2,1)S(1)} %copy-done), kind=kOutput, calls=%fused_computation.26 | convolution fusion | flops 1610612736 | bytes 6815744 | tf_op jit(solution)/shard_map/dot_general | solution.py:76
  158.7 5.0 %fusion.20 = bf16[1,1024,1024]{2,1,0:T(8,128)(2,1)} fusion(bf16[768,1024]{1,0:T(8,128)(2,1)} %bitcast.12, bf16[768,1024]{1,0:T(8,128)(2,1)} %copy-done.3), kind=kOutput, calls=%fused_computation.27 | convolution fusion | flops 1612709888 | bytes 5242880 | tf_op jit(solution)/shard_map/dot_general | solution.py:95
  163.7 31.9 %reduce-scatter.2.cloned.1.call-done = f32[256,768]{0,1:T(8,128)} async-done(((f32[1024,768]{0,1:T(8,128)}), f32[256,768]{0,1:T(8,128)}) %reduce-scatter.2.cloned.1.call-update) | async-done | bytes 786448 | tf_op jit(solution)/shard_map/reduce_scatter | solution.py:75
  195.7 1.9 convert_element_type.61
  197.6 5.5 %all-to-all-start.2 = ((bf16[256,8,96]{0,2,1:T(8,128)(2,1)}), bf16[256,8,96]{0,2,1:T(8,128)(2,1)S(1)}, u32[]{:S(2)}, u32[]{:S(2)}) async-start(bf16[256,8,96]{0,2,1:T(8,128)(2,1)} %bitcast.15), calls=%async_computation.3 | async-start | bytes 786432 | tf_op jit(solution)/shard_map/all_to_all | solution.py:83
  203.1 8.6 %fusion.3 = bf16[1,1024,2048]{2,1,0:T(8,128)(2,1)} fusion(bf16[768,2048]{1,0:T(8,128)(2,1)} %bitcast.9, f32[768,1024]{1,0:T(8,128)} %fusion.15), kind=kOutput, calls=%fused_computation.13 | convolution fusion | flops 3232497664 | bytes 10485760 | tf_op jit(solution)/shard_map/dot_general | solution.py:98
  211.7 2.9 %all-to-all-done.2 = bf16[256,8,96]{0,2,1:T(8,128)(2,1)S(1)} async-done(((bf16[256,8,96]{0,2,1:T(8,128)(2,1)}), bf16[256,8,96]{0,2,1:T(8,128)(2,1)S(1)}, u32[]{:S(2)}, u32[]{:S(2)}) %all-to-all-start.2) | async-done | bytes 393248 | tf_op jit(solution)/shard_map/all_to_all | solution.py:83
  214.6 1.9 gather_fusion.3
  216.7 1.3 reduce.1
  (23 shorter events, 0.6 us)
Async XLA Ops:
  7.2 67.7 %copy-start = (bf16[1,1024,1024]{2,1,0:T(8,128)(2,1)S(1)}, bf16[1,1024,1024]{2,1,0:T(8,128)(2,1)}, u32[]{:S(2)}) copy-start(bf16[1,1024,1024]{2,1,0:T(8,128)(2,1)} %param.10) | copy-start | bytes 6291460
  7.2 12.2 %copy-start.2 = (bf16[256,1024]{1,0:T(8,128)(2,1)S(1)}, bf16[256,1024]{1,0:T(8,128)(2,1)}, u32[]{:S(2)}) copy-start(bf16[256,1024]{1,0:T(8,128)(2,1)} %param.6) | copy-start | bytes 1572868
  23.0 10.2 %copy-start.1 = (bf16[256,2048]{1,0:T(8,128)(2,1)S(1)}, bf16[256,2048]{1,0:T(8,128)(2,1)}, u32[]{:S(2)}) copy-start(bf16[256,2048]{1,0:T(8,128)(2,1)} %param.7) | copy-start | bytes 3145732
  25.8 44.4 %all-to-all-start.1 = ((bf16[8,96,1024]{2,1,0:T(8,128)(2,1)}), bf16[8,96,1024]{2,1,0:T(8,128)(2,1)}, u32[]{:S(2)}, u32[]{:S(2)}) async-start(bf16[8,96,1024]{2,1,0:T(8,128)(2,1)} %broadcast_multiply_fusion), calls=%async_computation.1 | async-start | bytes 3145728 | tf_op jit(solution)/shard_map/all_to_all | solution.py:52
  70.2 74.6 %all-to-all-start = ((bf16[8,96,2048]{2,1,0:T(8,128)(2,1)}), bf16[8,96,2048]{2,1,0:T(8,128)(2,1)}, u32[]{:S(2)}, u32[]{:S(2)}) async-start(bf16[8,96,2048]{2,1,0:T(8,128)(2,1)} %fusion), calls=%async_computation | async-start | bytes 6291456 | tf_op jit(solution)/shard_map/all_to_all | solution.py:53
  74.6 121.0 %reduce-scatter.2.cloned.1.call-start = ((), (), s32[]{:S(2)}) async-start(), calls=%async_computation.4 | async-start | bytes 3932160 | tf_op jit(solution)/shard_map/reduce_scatter | solution.py:75
  153.9 1.2 copy-start.3
  197.6 17.0 %all-to-all-start.2 = ((bf16[256,8,96]{0,2,1:T(8,128)(2,1)}), bf16[256,8,96]{0,2,1:T(8,128)(2,1)S(1)}, u32[]{:S(2)}, u32[]{:S(2)}) async-start(bf16[256,8,96]{0,2,1:T(8,128)(2,1)} %bitcast.15), calls=%async_computation.3 | async-start | bytes 786432 | tf_op jit(solution)/shard_map/all_to_all | solution.py:83
Sparse Core Ops, SparseCore 0:
  158.8 36.8 reduce-scatter.1
where the time goes:
time: 225 us
  waiting for transfers between devices  129 us (57%)
  matrix products  31.2 us (14%)
  local copies, waits for them, and re-layouts  20.6 us (9%)
  starting transfers between devices  17.4 us (8%)
  between operations  14.2 us (6%)
  other arithmetic  12.9 us (6%)
    all_to_all x1, waiting for transfers between devices, shards(): lax.all_to_all(packed_dy, 'ep', split_axis=0, concat_axis=0, tiled=True)  65.1 us
    reduce_scatter x1, waiting for transfers between devices, shards(): lax.psum_scatter(lax.dot_general(weight_in, back_pre, (((1,), (1,)), ((),...  31.9 us
    all_to_all x1, waiting for transfers between devices, shards(): lax.all_to_all(packed_x, 'ep', split_axis=0, concat_axis=0, tiled=True)  28.7 us
    dot_general x1, matrix products, shards(): lax.dot_general(rows_dy, weight_out, (((1,), (1,)), ((), ())), preferred_...  9.11 us
    dot_general x1, matrix products, span_grads(): lax.dot_general(act_cols, rows_dy, (((0,), (0,)), ((), ())), preferred_el...  8.64 us
    all_to_all x1, starting transfers between devices, shards(): lax.all_to_all(packed_x, 'ep', split_axis=0, concat_axis=0, tiled=True)  7.28 us
    all_to_all x1, starting transfers between devices, shards(): lax.all_to_all(summed.astype(jnp.bfloat16), 'ep', split_axis=1, concat_ax...  5.49 us
    dot_general x1, matrix products, span_grads(): lax.dot_general(pre_cols, rows_x, (((0,), (0,)), ((), ())), preferred_ele...  5.04 us
  transfers between devices with their start and end apart: 4, of which 4 were waited for; matrix products, arithmetic and copies ran while one was open for 12% of the time, Pallas kernels for 0%

commit v1 on v0

--- a/solution.py
+++ b/solution.py
@@ -5,6 +5,29 @@
 from jax.sharding import PartitionSpec as P
 
 E = 8
+
+
+def split_up(shard, dim, devices):
+    before, after = (shard.shape[:dim], shard.shape[dim + 1 :])
+    return jnp.moveaxis(shard.reshape(*before, devices, -1, *after), dim, 0)
+
+
+def joined_along(parts, dim):
+    lengths = list(parts.shape[1:])
+    lengths[dim] *= parts.shape[0]
+    return jnp.moveaxis(parts, 0, dim).reshape(lengths)
+
+
+def sent_to_each(x, axis, split_dim, concat_dim):
+    length, place = (lax.axis_size(axis), lax.axis_index(axis))
+    tiles = split_up(x, split_dim, length)
+    whole = tiles
+    for step in range(1, length):
+        target, source = ((place + step) % length, (place - step) % length)
+        sent = lax.dynamic_index_in_dim(tiles, target, 0)
+        partner_block = lax.ppermute(sent, axis, [(i, (i + step) % length) for i in range(length)])
+        whole = lax.dynamic_update_slice_in_dim(whole, partner_block, source, axis=0)
+    return joined_along(whole, concat_dim)
 
 
 def shifted(value, axis, by):
@@ -80,9 +103,7 @@
         scatter_dimension=0,
         tiled=True,
     )
-    returned = lax.all_to_all(
-        summed.astype(jnp.bfloat16), "ep", split_axis=1, concat_axis=1, tiled=True
-    )
+    returned = sent_to_each(summed.astype(jnp.bfloat16), "ep", 1, 1)
     picked = returned[:, positions].astype(jnp.float32)
     grad_in = jnp.sum(picked.reshape(picked.shape[0], tokens_here, 2), axis=2).T.astype(
         jnp.bfloat16

time: 225 us -> 228 us (1.013)
  starting transfers between devices: 17.4 us -> 24.4 us
  waiting for transfers between devices: 129 us -> 124 us
    ppermute x0 -> x7, starting transfers between devices: none -> 12.4 us  [sent_to_each(): lax.ppermute(sent, axis, [(i, (i + step) % length) for i in range(length)])]
    all_to_all x1 -> x0, starting transfers between devices: 5.49 us -> none  [shards(): lax.all_to_all(summed.astype(jnp.bfloat16), 'ep', split_axis=1, concat_ax...]
    reduce_scatter x1, waiting for transfers between devices: 31.9 us -> 28 us  [shards(): lax.psum_scatter(lax.dot_general(weight_in, back_pre, (((1,), (1,)), ((),...]
    all_to_all x1 -> x0, waiting for transfers between devices: 2.92 us -> none  [shards(): lax.all_to_all(summed.astype(jnp.bfloat16), 'ep', split_axis=1, concat_ax...]
    ppermute x0 -> x7, waiting for transfers between devices: none -> 2.54 us  [sent_to_each(): lax.ppermute(sent, axis, [(i, (i + step) % length) for i in range(length)])]
  transfers between devices with their start and end apart: 4 -> 10, of which waited for: 4 -> 5; matrix products, arithmetic and copies ran while one was open for 12% -> 12% of each run, Pallas kernels for 0% -> 0%
where the time goes in v1:
time: 228 us; the launch traced here: 227 us
  waiting for transfers between devices  124 us (54%)
  matrix products  31.2 us (14%)
  starting transfers between devices  24.4 us (11%)
  local copies, waits for them, and re-layouts  20.4 us (9%)
  between operations  14.5 us (6%)
  other arithmetic  12.3 us (5%)
    all_to_all x1, waiting for transfers between devices, shards(): lax.all_to_all(packed_dy, 'ep', split_axis=0, concat_axis=0, tiled=True)  65.1 us
    all_to_all x1, waiting for transfers between devices, shards(): lax.all_to_all(packed_x, 'ep', split_axis=0, concat_axis=0, tiled=True)  28.7 us
    reduce_scatter x1, waiting for transfers between devices, shards(): lax.psum_scatter(lax.dot_general(weight_in, back_pre, (((1,), (1,)), ((),...  28 us
    ppermute x7, starting transfers between devices, sent_to_each(): lax.ppermute(sent, axis, [(i, (i + step) % length) for i in range(length)])  12.4 us
    dot_general x1, matrix products, shards(): lax.dot_general(rows_dy, weight_out, (((1,), (1,)), ((), ())), preferred_...  9.11 us
    dot_general x1, matrix products, span_grads(): lax.dot_general(act_cols, rows_dy, (((0,), (0,)), ((), ())), preferred_el...  8.64 us
    all_to_all x1, starting transfers between devices, shards(): lax.all_to_all(packed_x, 'ep', split_axis=0, concat_axis=0, tiled=True)  7.28 us
    dot_general x1, matrix products, span_grads(): lax.dot_general(pre_cols, rows_x, (((0,), (0,)), ((), ())), preferred_ele...  5.04 us
  transfers between devices with their start and end apart: 10, of which 5 were waited for; matrix products, arithmetic and copies ran while one was open for 12% of the time, Pallas kernels for 0%

profile of v1, /device:TPU:0, one launch (start us, length us, event | category | flops | bytes accessed | tf_op | source)
XLA Modules:
  0.0 227.1 jit_solution(11038511847428930730)
XLA Ops:
  7.2 0.8 broadcast_multiply_fusion.1
  8.0 0.8 copy.10
  9.3 1.1 reduce-window.6
  10.8 2.4 %scatter_custom_fusion = s32[768]{0:T(1024)S(1)} fusion(s32[512]{0:T(512)S(1)} %bitcast.77, s32[512]{0:T(512)S(1)} %iota.15, s32[]{:T(128)} %constant.145.clone.1), kind=kCustom, calls=%fused_computation.71 | custom fusion | bytes 3076 | tf_op jit(solution)/shard_map/scatter | solution.py:62
  14.3 5.0 %gather_fusion.1 = f32[768]{0:T(1024)S(1)} fusion(f32[512]{0:T(512)S(1)} %div.25, s32[1024]{0:T(1024)S(1)} %get-tuple-element.14), kind=kCustom, calls=%fused_computation.1 | custom fusion | bytes 9216 | tf_op jit(solution)/shard_map/gather | solution.py:68
  19.4 3.5 %gather_fusion.2 = bf16[768,1024]{1,0:T(8,128)(2,1)} fusion(bf16[256,1024]{1,0:T(8,128)(2,1)S(1)} %copy-done.2, s32[1024]{0:T(1024)S(1)} %get-tuple-element.15), kind=kCustom, calls=%fused_computation.2 | custom fusion | bytes 3148800 | tf_op jit(solution)/shard_map/gather | solution.py:70
  23.0 2.8 %broadcast_multiply_fusion = bf16[8,96,1024]{2,1,0:T(8,128)(2,1)} fusion(bf16[8,96,1024]{2,1,0:T(8,128)(2,1)} %bitcast.74, bf16[8,96]{1,0:T(8,128)(2,1)S(1)} %reshape.209), kind=kLoop, calls=%fused_computation.32 | loop fusion | flops 786432 | bytes 3147264 | tf_op jit(solution)/shard_map/mul | solution.py:70
  25.8 7.3 %all-to-all-start.1 = ((bf16[8,96,1024]{2,1,0:T(8,128)(2,1)}), bf16[8,96,1024]{2,1,0:T(8,128)(2,1)}, u32[]{:S(2)}, u32[]{:S(2)}) async-start(bf16[8,96,1024]{2,1,0:T(8,128)(2,1)} %broadcast_multiply_fusion), calls=%async_computation.1 | async-start | bytes 3145728 | tf_op jit(solution)/shard_map/all_to_all | solution.py:75
  33.1 4.2 %gather_fusion = bf16[768,2048]{1,0:T(8,128)(2,1)} fusion(bf16[256,2048]{1,0:T(8,128)(2,1)S(1)} %copy-done.1, s32[1024]{0:T(1024)S(1)} %get-tuple-element.15), kind=kCustom, calls=%fused_computation | custom fusion | bytes 6294528 | tf_op jit(solution)/shard_map/gather | solution.py:71
  37.4 4.1 %fusion = bf16[8,96,2048]{2,1,0:T(8,128)(2,1)} fusion(bf16[8,96,2048]{2,1,0:T(8,128)(2,1)} %bitcast.73, f32[8,96]{1,0:T(8,128)S(1)} %mul.111), kind=kLoop, calls=%fused_computation.7 | loop fusion | flops 4718592 | bytes 6294528 | tf_op jit(solution)/shard_map/convert_element_type | solution.py:71
  41.5 28.7 %all-to-all-done.1 = bf16[8,96,1024]{2,1,0:T(8,128)(2,1)} async-done(((bf16[8,96,1024]{2,1,0:T(8,128)(2,1)}), bf16[8,96,1024]{2,1,0:T(8,128)(2,1)}, u32[]{:S(2)}, u32[]{:S(2)}) %all-to-all-start.1) | async-done | bytes 1572896 | tf_op jit(solution)/shard_map/all_to_all | solution.py:75
  70.2 4.5 %all-to-all-start = ((bf16[8,96,2048]{2,1,0:T(8,128)(2,1)}), bf16[8,96,2048]{2,1,0:T(8,128)(2,1)}, u32[]{:S(2)}, u32[]{:S(2)}) async-start(bf16[8,96,2048]{2,1,0:T(8,128)(2,1)} %fusion), calls=%async_computation | async-start | bytes 6291456 | tf_op jit(solution)/shard_map/all_to_all | solution.py:76
  74.9 4.9 %fusion.15 = f32[768,1024]{1,0:T(8,128)} fusion(bf16[768,1024]{1,0:T(8,128)(2,1)} %bitcast.12, bf16[1,1024,1024]{2,1,0:T(8,128)(2,1)S(1)} %copy-done), kind=kOutput, calls=%fused_computation.24 | convolution fusion | flops 1610612736 | bytes 6815744 | tf_op jit(solution)/shard_map/dot_general | solution.py:91
  79.8 65.1 %all-to-all-done = bf16[8,96,2048]{2,1,0:T(8,128)(2,1)} async-done(((bf16[8,96,2048]{2,1,0:T(8,128)(2,1)}), bf16[8,96,2048]{2,1,0:T(8,128)(2,1)}, u32[]{:S(2)}, u32[]{:S(2)}) %all-to-all-start) | async-done | bytes 3145760 | tf_op jit(solution)/shard_map/all_to_all | solution.py:76
  144.8 9.1 %fusion.10 = bf16[768,1024]{1,0:T(8,128)(2,1)S(1)} fusion(f32[768,1024]{1,0:T(8,128)} %fusion.15, bf16[768,2048]{1,0:T(8,128)(2,1)} %bitcast.9, bf16[1,1024,2048]{2,1,0:T(8,128)(2,1)} %param.11), kind=kOutput, calls=%fused_computation.20 | convolution fusion | flops 3236954112 | bytes 12058624 | tf_op jit(solution)/shard_map/dot_general | solution.py:94
  153.9 1.1 copy-done.3
  155.1 3.5 %fusion.17 = f32[1024,768]{0,1:T(8,128)} fusion(bf16[768,1024]{1,0:T(8,128)(2,1)S(1)} %fusion.10, bf16[1,1024,1024]{2,1,0:T(8,128)(2,1)S(1)} %copy-done), kind=kOutput, calls=%fused_computation.26 | convolution fusion | flops 1610612736 | bytes 6815744 | tf_op jit(solution)/shard_map/dot_general | solution.py:99
  158.9 8.6 %fusion.3 = bf16[1,1024,2048]{2,1,0:T(8,128)(2,1)} fusion(bf16[768,2048]{1,0:T(8,128)(2,1)} %bitcast.9, f32[768,1024]{1,0:T(8,128)} %fusion.15), kind=kOutput, calls=%fused_computation.13 | convolution fusion | flops 3232497664 | bytes 10485760 | tf_op jit(solution)/shard_map/dot_general | solution.py:119
  167.5 28.0 %reduce-scatter.2.cloned.1.call-done = f32[256,768]{0,1:T(8,128)} async-done(((f32[1024,768]{0,1:T(8,128)}), f32[256,768]{0,1:T(8,128)}) %reduce-scatter.2.cloned.1.call-update) | async-done | bytes 786448 | tf_op jit(solution)/shard_map/reduce_scatter | solution.py:98
  195.6 1.2 convert_element_type.61
  196.8 1.8 collective-permute-start
  198.6 5.0 %fusion.20 = bf16[1,1024,1024]{2,1,0:T(8,128)(2,1)} fusion(bf16[768,1024]{1,0:T(8,128)(2,1)} %bitcast.12, bf16[768,1024]{1,0:T(8,128)(2,1)} %copy-done.3), kind=kOutput, calls=%fused_computation.27 | convolution fusion | flops 1612709888 | bytes 5242880 | tf_op jit(solution)/shard_map/dot_general | solution.py:116
  203.6 1.5 collective-permute-start.1
  205.1 2.4 %collective-permute-start.2 = (bf16[1,256,96]{1,2,0:T(8,128)(2,1)S(1)}, bf16[1,256,96]{1,2,0:T(8,128)(2,1)S(1)}, u32[]{:S(2)}, u32[]{:S(2)}) collective-permute-start(bf16[1,256,96]{1,2,0:T(8,128)(2,1)S(1)} %get-tuple-element.9), channel_id=1, source_target_pairs={{0,12},{4,16},{8,20},{12,24},{16,28},{20,0},{24,4},{28,8},{1,13},{... | collective-permute-start | bytes 147464 | tf_op jit(solution)/shard_map/ppermute | solution.py:28
  207.5 1.4 collective-permute-start.3
  208.9 2.4 %collective-permute-start.4 = (bf16[1,256,96]{1,2,0:T(8,128)(2,1)S(1)}, bf16[1,256,96]{1,2,0:T(8,128)(2,1)S(1)}, u32[]{:S(2)}, u32[]{:S(2)}) collective-permute-start(bf16[1,256,96]{1,2,0:T(8,128)(2,1)S(1)} %get-tuple-element.7), channel_id=1, source_target_pairs={{0,20},{4,24},{8,28},{12,0},{16,4},{20,8},{24,12},{28,16},{1,21},{... | collective-permute-start | bytes 147464 | tf_op jit(solution)/shard_map/ppermute | solution.py:28
  211.3 1.4 collective-permute-start.5
  212.8 1.5 collective-permute-start.6
  214.4 1.4 collective-permute-done.5
  215.8 1.1 collective-permute-done.6
  216.9 1.9 gather_fusion.3
  219.0 1.3 reduce.1
  (43 shorter events, 2.4 us)
Async XLA Ops:
  7.2 67.7 %copy-start = (bf16[1,1024,1024]{2,1,0:T(8,128)(2,1)S(1)}, bf16[1,1024,1024]{2,1,0:T(8,128)(2,1)}, u32[]{:S(2)}) copy-start(bf16[1,1024,1024]{2,1,0:T(8,128)(2,1)} %param.10) | copy-start | bytes 6291460
  7.2 12.2 %copy-start.2 = (bf16[256,1024]{1,0:T(8,128)(2,1)S(1)}, bf16[256,1024]{1,0:T(8,128)(2,1)}, u32[]{:S(2)}) copy-start(bf16[256,1024]{1,0:T(8,128)(2,1)} %param.6) | copy-start | bytes 1572868
  23.0 10.1 %copy-start.1 = (bf16[256,2048]{1,0:T(8,128)(2,1)S(1)}, bf16[256,2048]{1,0:T(8,128)(2,1)}, u32[]{:S(2)}) copy-start(bf16[256,2048]{1,0:T(8,128)(2,1)} %param.7) | copy-start | bytes 3145732
  25.8 44.4 %all-to-all-start.1 = ((bf16[8,96,1024]{2,1,0:T(8,128)(2,1)}), bf16[8,96,1024]{2,1,0:T(8,128)(2,1)}, u32[]{:S(2)}, u32[]{:S(2)}) async-start(bf16[8,96,1024]{2,1,0:T(8,128)(2,1)} %broadcast_multiply_fusion), calls=%async_computation.1 | async-start | bytes 3145728 | tf_op jit(solution)/shard_map/all_to_all | solution.py:75
  70.2 74.6 %all-to-all-start = ((bf16[8,96,2048]{2,1,0:T(8,128)(2,1)}), bf16[8,96,2048]{2,1,0:T(8,128)(2,1)}, u32[]{:S(2)}, u32[]{:S(2)}) async-start(bf16[8,96,2048]{2,1,0:T(8,128)(2,1)} %fusion), calls=%async_computation | async-start | bytes 6291456 | tf_op jit(solution)/shard_map/all_to_all | solution.py:76
  74.6 120.9 %reduce-scatter.2.cloned.1.call-start = ((), (), s32[]{:S(2)}) async-start(), calls=%async_computation.3 | async-start | bytes 3932160 | tf_op jit(solution)/shard_map/reduce_scatter | solution.py:98
  153.9 1.1 copy-start.3
  196.8 14.5 %collective-permute-start = (bf16[1,256,96]{1,2,0:T(8,128)(2,1)S(1)}, bf16[1,256,96]{1,2,0:T(8,128)(2,1)S(1)}, u32[]{:S(2)}, u32[]{:S(2)}) collective-permute-start(bf16[1,256,96]{1,2,0:T(8,128)(2,1)S(1)} %get-tuple-element.11), channel_id=1, source_target_pairs={{0,4},{4,8},{8,12},{12,16},{16,20},{20,24},{24,28},{28,0},{1,5},{5... | collective-permute-start | bytes 147464 | tf_op jit(solution)/shard_map/ppermute | solution.py:28
  203.6 9.2 %collective-permute-start.1 = (bf16[1,256,96]{1,2,0:T(8,128)(2,1)S(1)}, bf16[1,256,96]{1,2,0:T(8,128)(2,1)S(1)}, u32[]{:S(2)}, u32[]{:S(2)}) collective-permute-start(bf16[1,256,96]{1,2,0:T(8,128)(2,1)S(1)} %get-tuple-element.10), channel_id=1, source_target_pairs={{0,8},{4,12},{8,16},{12,20},{16,24},{20,28},{24,0},{28,4},{1,9},{5... | collective-permute-start | bytes 147464 | tf_op jit(solution)/shard_map/ppermute | solution.py:28
  205.1 9.2 %collective-permute-start.2 = (bf16[1,256,96]{1,2,0:T(8,128)(2,1)S(1)}, bf16[1,256,96]{1,2,0:T(8,128)(2,1)S(1)}, u32[]{:S(2)}, u32[]{:S(2)}) collective-permute-start(bf16[1,256,96]{1,2,0:T(8,128)(2,1)S(1)} %get-tuple-element.9), channel_id=1, source_target_pairs={{0,12},{4,16},{8,20},{12,24},{16,28},{20,0},{24,4},{28,8},{1,13},{... | collective-permute-start | bytes 147464 | tf_op jit(solution)/shard_map/ppermute | solution.py:28
  207.5 6.8 %collective-permute-start.3 = (bf16[1,256,96]{1,2,0:T(8,128)(2,1)S(1)}, bf16[1,256,96]{1,2,0:T(8,128)(2,1)S(1)}, u32[]{:S(2)}, u32[]{:S(2)}) collective-permute-start(bf16[1,256,96]{1,2,0:T(8,128)(2,1)S(1)} %get-tuple-element.8), channel_id=1, source_target_pairs={{0,16},{4,20},{8,24},{12,28},{16,0},{20,4},{24,8},{28,12},{1,17},{... | collective-permute-start | bytes 147464 | tf_op jit(solution)/shard_map/ppermute | solution.py:28
  208.9 5.5 %collective-permute-start.4 = (bf16[1,256,96]{1,2,0:T(8,128)(2,1)S(1)}, bf16[1,256,96]{1,2,0:T(8,128)(2,1)S(1)}, u32[]{:S(2)}, u32[]{:S(2)}) collective-permute-start(bf16[1,256,96]{1,2,0:T(8,128)(2,1)S(1)} %get-tuple-element.7), channel_id=1, source_target_pairs={{0,20},{4,24},{8,28},{12,0},{16,4},{20,8},{24,12},{28,16},{1,21},{... | collective-permute-start | bytes 147464 | tf_op jit(solution)/shard_map/ppermute | solution.py:28
  211.3 4.5 %collective-permute-start.5 = (bf16[1,256,96]{1,2,0:T(8,128)(2,1)S(1)}, bf16[1,256,96]{1,2,0:T(8,128)(2,1)S(1)}, u32[]{:S(2)}, u32[]{:S(2)}) collective-permute-start(bf16[1,256,96]{1,2,0:T(8,128)(2,1)S(1)} %get-tuple-element.6), channel_id=1, source_target_pairs={{0,24},{4,28},{8,0},{12,4},{16,8},{20,12},{24,16},{28,20},{1,25},{... | collective-permute-start | bytes 147464 | tf_op jit(solution)/shard_map/ppermute | solution.py:28
  212.8 4.1 %collective-permute-start.6 = (bf16[1,256,96]{1,2,0:T(8,128)(2,1)S(1)}, bf16[1,256,96]{1,2,0:T(8,128)(2,1)S(1)}, u32[]{:S(2)}, u32[]{:S(2)}) collective-permute-start(bf16[1,256,96]{1,2,0:T(8,128)(2,1)S(1)} %get-tuple-element.5), channel_id=1, source_target_pairs={{0,28},{4,0},{8,4},{12,8},{16,12},{20,16},{24,20},{28,24},{1,29},{... | collective-permute-start | bytes 147464 | tf_op jit(solution)/shard_map/ppermute | solution.py:28
Sparse Core Ops, SparseCore 0:
  158.7 36.7 reduce-scatter.1
